TPU v7x, 512 devices: a whole 4x8x8 slice. The times are simulated.
512 devices in a mesh: rep: 32 (over x, z), tp: 16 (over y, core).
Axes of the slice: x: 4, y: 8, z: 8, core: 2. Of those that a mesh axis runs over, the one named last changes fastest.
Arguments:
- queries: bfloat16 [10240, 8192], P('rep', 'tp'), may hold values from -30 to 30
- fresh_kv: bfloat16 [10240, 4096], P('rep', 'tp'), may hold values from -6 to 6, as said below
- kv_cache: bfloat16 [1408, 16, 8, 256], P('rep', 'tp'), may hold values from -6 to 6, as said below
- cached_len: int32 [640], P('rep'), may hold values from 1 to 48, as said below
- page_table: int32 [640, 6], P('rep'), may hold values from 0 to 43, as said below
- out_weight: bfloat16 [8192, 4096], P('tp'), may hold values from -0.09375 to 0.09375
- adapter_down: bfloat16 [64, 64, 8192], P('rep', None, 'tp'), may hold values from -0.0625 to 0.0625
- pooled_up_weight: bfloat16 [64, 64, 4096], P('rep', None, 'tp'), may hold values from -0.75 to 0.75
- adapter_ids: int32 [640], P('rep'), may hold values from 0 to 63, as said below
- pool_slot: int32 [64], replicated, may hold values from 0 to 63, as said below
Outputs:
- adapted_output: bfloat16 [10240, 4096], P('rep', 'tp')
Inputs may be any that keep to these rules, and one draw needn't show every extreme that they name: `kv_cache`: slots that hold the same key-value head are equal. `fresh_kv`: slots that hold the same key-value head are equal. `cached_len`: A row with cached length n uses its first ceil(n / 8) page table entries; in every replica some row has 48. `page_table`: entries index the 44 pages of the row's own replica. The pages that a row uses are distinct, no page is used by two rows of one replica, every page of a replica is used, and entries past a row's used pages repeat its first page. `adapter_ids`: row r of replica i is entry i * 20 + r. The owner of adapter a is replica pool_slot[a] // 2. Within one replica at most 2 rows name adapters of one owner, and one owner, the same for all replicas, is named by exactly 2 rows of every replica. A permutation: adapter a's blocks are adapter_down[pool_slot[a]] and pooled_up_weight[pool_slot[a]].
All inputs are finite; a program needn't handle non-finite values.
Results may differ from a plain program's by a relative error of at most 0.023.
Values may be sent and summed in bfloat16 or wider, within the bound.
No kernel may reach another device: no remote copies, remote signals or barrier semaphores. Data moves between devices by JAX's collectives and lax.ppermute only.
A program may use at most 64 MiB of HBM per device.

v0:
```python
import math
import jax
import jax.numpy as jnp
from jax import lax
from jax.sharding import PartitionSpec as P

ADAPTER_SCALE = 2.0


def shards(
    queries,
    fresh_kv,
    kv_cache,
    cached_len,
    page_table,
    out_weight,
    adapter_down,
    pooled_up_weight,
    adapter_ids,
    pool_slot,
):
    row_count = cached_len.shape[0]
    token_count = queries.shape[0]
    per_row = token_count // row_count
    slot_count = kv_cache.shape[1]
    page_len = kv_cache.shape[2]
    head_dim = kv_cache.shape[3] // 2
    feat_width = queries.shape[1]
    head_count = feat_width // head_dim
    heads_per_slot = head_count // slot_count
    cache_span = page_table.shape[1] * page_len
    output_columns = pooled_up_weight.shape[2]
    rank_size = adapter_down.shape[1]
    paged_kv = (
        kv_cache[page_table]
        .transpose(0, 2, 1, 3, 4)
        .reshape(row_count, slot_count, cache_span, 2 * head_dim)
    )
    recent = fresh_kv.reshape(row_count, per_row, slot_count, 2 * head_dim).transpose(0, 2, 1, 3)
    entries = jnp.concatenate([paged_kv, recent], axis=2)
    key_part = entries[..., :head_dim]
    value_part = entries[..., head_dim:]
    query_rows = queries.reshape(
        row_count, per_row, slot_count, heads_per_slot, head_dim
    ).transpose(0, 2, 1, 3, 4)
    query_rows = query_rows.reshape(row_count, slot_count, per_row * heads_per_slot, head_dim)
    scores = jnp.einsum(
        "rsad,rskd->rsak", query_rows, key_part, preferred_element_type=jnp.float32
    ) / math.sqrt(head_dim)
    entry_ids = jnp.arange(cache_span + per_row)[None, None, None, :]
    token_ids = (jnp.arange(per_row * heads_per_slot) // heads_per_slot)[None, None, :, None]
    allowed = jnp.where(
        entry_ids < cache_span,
        entry_ids < cached_len[:, None, None, None],
        entry_ids - cache_span <= token_ids,
    )
    scores = jnp.where(allowed, scores, -jnp.inf)
    peak_score = jnp.max(scores, axis=-1, keepdims=True)
    raised = jnp.exp(scores - peak_score)
    weights = (raised / jnp.sum(raised, axis=-1, keepdims=True)).astype(jnp.bfloat16)
    attended = jnp.einsum(
        "rsak,rskd->rsad", weights, value_part, preferred_element_type=jnp.float32
    ).astype(jnp.bfloat16)
    attended = attended.reshape(row_count, slot_count, per_row, heads_per_slot, head_dim).transpose(
        0, 2, 1, 3, 4
    )
    attended = attended.reshape(token_count, feat_width)
    plain_output = (
        lax.psum_scatter(
            lax.dot_general(
                out_weight, attended, (((0,), (1,)), ((), ())), preferred_element_type=jnp.float32
            ).astype(jnp.bfloat16),
            "tp",
            scatter_dimension=0,
            tiled=True,
        )
        .astype(jnp.float32)
        .T
    )
    slot_hits = adapter_ids[:, None] == jnp.arange(pool_slot.shape[0])[None, :]
    pool_position = jnp.sum(jnp.where(slot_hits, pool_slot[None, :], 0), axis=1)
    by_row = attended.reshape(row_count, per_row, feat_width)
    replicas = lax.axis_size("rep")
    local_count = adapter_down.shape[0]
    capacity = (row_count + replicas - 1) // replicas + 1
    owner_of = pool_position // local_count
    local_slot = pool_position % local_count
    same_owner = owner_of[:, None] == owner_of[None, :]
    earlier = jnp.arange(row_count)[None, :] < jnp.arange(row_count)[:, None]
    seat_of = jnp.sum(same_owner & earlier, axis=1)
    target = owner_of * capacity + seat_of
    placing = jnp.arange(replicas * capacity)[:, None] == target[None, :]
    placing_mat = placing.astype(jnp.bfloat16)
    wanted = (jnp.sum(jnp.where(placing, local_slot[None, :] + 1, 0), axis=1) - 1).reshape(
        replicas, capacity
    )
    choose = (
        lax.all_to_all(wanted, "rep", split_axis=0, concat_axis=0, tiled=True)[:, :, None]
        == jnp.arange(local_count)[None, None, :]
    ).astype(jnp.bfloat16)
    down_blocks = jnp.einsum(
        "smj,jkf->smkf", choose, adapter_down, preferred_element_type=jnp.float32
    ).astype(jnp.bfloat16)
    up_blocks = jnp.einsum(
        "smj,jkd->smkd", choose, pooled_up_weight, preferred_element_type=jnp.float32
    ).astype(jnp.bfloat16)
    down_got = lax.all_to_all(down_blocks, "rep", split_axis=0, concat_axis=0, tiled=True)
    up_got = lax.all_to_all(up_blocks, "rep", split_axis=0, concat_axis=0, tiled=True)
    down_got = down_got.reshape(replicas * capacity, rank_size, feat_width)
    up_got = up_got.reshape(replicas * capacity, rank_size, output_columns)
    down_sel = jnp.einsum(
        "sr,skf->rkf", placing_mat, down_got, preferred_element_type=jnp.float32
    ).astype(jnp.bfloat16)
    up_sel = jnp.einsum(
        "sr,skd->rkd", placing_mat, up_got, preferred_element_type=jnp.float32
    ).astype(jnp.bfloat16)
    shrink_part = jnp.einsum("rqf,rkf->rqk", by_row, down_sel, preferred_element_type=jnp.float32)
    down_projected = lax.psum(shrink_part.astype(jnp.bfloat16), "tp")
    adapter_correction = jnp.einsum(
        "owe,oet->owt", down_projected, up_sel, preferred_element_type=jnp.float32
    ).astype(jnp.bfloat16)
    adapted_output = plain_output + ADAPTER_SCALE * adapter_correction.reshape(
        token_count, output_columns
    ).astype(jnp.float32)
    return adapted_output.astype(jnp.bfloat16)


def solution(mesh):
    return jax.shard_map(
        shards,
        mesh=mesh,
        in_specs=(
            P("rep", "tp"),
            P("rep", "tp"),
            P("rep", "tp", None, None),
            P("rep"),
            P("rep", None),
            P("tp", None),
            P("rep", None, "tp"),
            P("rep", None, "tp"),
            P("rep"),
            P(),
        ),
        out_specs=P("rep", "tp"),
        check_vma=False,
    )
```

profile of v0, /device:TPU:64, one launch (start us, length us, event | category | flops | bytes accessed | tf_op | source)
XLA Modules:
  0.0 253.9 jit_solution(10275384888598889129)
XLA Ops:
  6.5 0.0 copy-start
  6.5 0.9 select_reduce_fusion.1
  7.4 0.2 convert_reduce_fusion
  7.6 0.1 select_reduce_fusion
  7.7 0.1 sub.34
  7.8 21.0 %all_to_all.16 = s32[32,1,2]{2,1,0:T(1,128)S(1)} all-to-all(s32[32,1,2]{2,1,0:T(1,128)S(1)} %bitcast.62), channel_id=1, replica_groups=mesh['rep'=32,'tp'=16] {'rep'}, dimensions={0} | all-to-all | bytes 512 | tf_op jit(solution)/shard_map/all_to_all | solution.py:98
  28.9 0.1 copy.38
  29.0 1.6 convolution_convert_fusion.2
  30.6 2.5 copy.44
  33.1 0.0 copy-start.2
  33.1 5.2 %all-to-all-start.2 = ((bf16[32,2,64,256]{3,2,1,0:T(8,128)(2,1)}), bf16[32,2,64,256]{3,2,1,0:T(8,128)(2,1)S(1)}, u32[]{:S(2)}, u32[]{:S(2)}) async-start(bf16[32,2,64,256]{3,2,1,0:T(8,128)(2,1)} %copy.44), calls=%async_computation.3 | async-start | bytes 4194304 | tf_op jit(solution)/shard_map/all_to_all | solution.py:108
  38.3 0.0 copy-done.2
  38.3 1.3 convolution_convert_fusion.1
  39.6 4.3 %copy.40 = bf16[32,2,64,512]{3,2,1,0:T(8,128)(2,1)} copy(bf16[32,2,64,512]{3,0,2,1:T(8,128)(2,1)S(1)} %convolution_convert_fusion.1) | data formatting | bytes 8388608 | tf_op jit(solution)/shard_map/convert_element_type | solution.py:103
  43.9 0.0 copy-start.3
  43.9 0.0 copy-start.1
  43.9 0.0 copy-start.4
  43.9 0.0 copy-start.5
  43.9 43.8 %all-to-all-done.2 = bf16[32,2,64,256]{3,2,1,0:T(8,128)(2,1)S(1)} async-done(((bf16[32,2,64,256]{3,2,1,0:T(8,128)(2,1)}), bf16[32,2,64,256]{3,2,1,0:T(8,128)(2,1)S(1)}, u32[]{:S(2)}, u32[]{:S(2)}) %all-to-all-start.2) | async-done | bytes 2097184 | tf_op jit(solution)/shard_map/all_to_all | solution.py:108
  87.7 5.8 %all-to-all-start.1 = ((bf16[32,2,64,512]{3,2,1,0:T(8,128)(2,1)}), bf16[32,2,64,512]{3,2,1,0:T(8,128)(2,1)}, u32[]{:S(2)}, u32[]{:S(2)}) async-start(bf16[32,2,64,512]{3,2,1,0:T(8,128)(2,1)} %copy.40), calls=%async_computation.2 | async-start | bytes 8388608 | tf_op jit(solution)/shard_map/all_to_all | solution.py:107
  93.5 0.2 reduce-scatter.2.cloned.1.call-start
  93.7 0.0 copy-done.3
  93.8 0.1 copy.35
  93.9 0.1 reshape.210
  93.9 0.0 copy-done.1
  94.0 0.2 reshape.202
  94.2 0.0 copy-done
  94.2 0.7 gather_fusion
  94.9 0.0 copy-done.4
  94.9 0.1 iota_compare_fusion.3
  95.0 0.1 broadcast_compare_fusion
  95.0 0.0 copy-done.5
  95.0 0.4 fusion.56
  95.5 1.2 fusion.17
  96.7 1.7 convolution_convert_fusion.3
  98.4 0.2 reshape_transpose_reshape.4
  98.6 5.4 %fusion.1 = bf16[4096,320]{0,1:T(8,128)(2,1)} fusion(bf16[320,512]{1,0:T(8,128)(2,1)S(1)} %reshape_transpose_reshape.4, bf16[512,4096]{1,0:T(8,128)(2,1)} %param.15), kind=kOutput, calls=%fused_computation.3 | convolution fusion | flops 1343488000 | bytes 7143424 | tf_op jit(solution)/shard_map/dot_general | solution.py:70
  104.0 0.0 reduce-scatter.2.cloned.1.call-update
  104.0 0.2 reshape_reshape_transpose_reshape.3
  104.2 1.3 fusion.9
  105.4 82.9 %all-to-all-done.1 = bf16[32,2,64,512]{3,2,1,0:T(8,128)(2,1)} async-done(((bf16[32,2,64,512]{3,2,1,0:T(8,128)(2,1)}), bf16[32,2,64,512]{3,2,1,0:T(8,128)(2,1)}, u32[]{:S(2)}, u32[]{:S(2)}) %all-to-all-start.1) | async-done | bytes 4194336 | tf_op jit(solution)/shard_map/all_to_all | solution.py:107
  188.4 6.7 %fusion.6 = bf16[20,64,512]{2,0,1:T(8,128)(2,1)S(1)} fusion(bf16[64,64,512]{2,1,0:T(8,128)(2,1)} %bitcast.14, s32[20]{0:T(128)S(1)} %multiply_add_fusion), kind=kOutput, calls=%fused_computation.10 | convolution fusion | flops 84542720 | bytes 5505104 | tf_op jit(solution)/shard_map/sr,skf->rkf/dot_general | solution.py:111
  195.1 0.5 fusion.20
  195.6 49.5 %psum.7 = bf16[20,16,64]{2,1,0:T(8,128)(2,1)S(1)} all-reduce(bf16[20,16,64]{2,1,0:T(8,128)(2,1)S(1)} %fusion.20), channel_id=1, replica_groups=mesh['rep'=32,'tp'=16] {'tp'}, use_global_device_ids=true, to_apply=%region_6.7 | all-reduce | flops 20480 | bytes 81920 | tf_op jit(solution)/shard_map/psum | solution.py:118
  245.1 0.2 fusion.19
  245.4 0.0 reduce-scatter.2.cloned.1.call-done
  245.4 1.6 fusion.30
  (7 shorter events, 0.0 us)
Async XLA Ops:
  6.5 87.7 %copy-start = (bf16[44,1,8,256]{3,2,1,0:T(8,128)(2,1)S(1)}, bf16[44,1,8,256]{3,2,1,0:T(8,128)(2,1)}, u32[]{:S(2)}) copy-start(bf16[44,1,8,256]{3,2,1,0:T(8,128)(2,1)} %param.12) | copy-start | bytes 540676
  33.1 5.2 %copy-start.2 = (bf16[2,64,512]{2,1,0:T(8,128)(2,1)S(1)}, bf16[2,64,512]{2,1,0:T(8,128)(2,1)}, u32[]{:S(2)}) copy-start(bf16[2,64,512]{2,1,0:T(8,128)(2,1)} %param.16) | copy-start | bytes 393220
  33.1 54.6 %all-to-all-start.2 = ((bf16[32,2,64,256]{3,2,1,0:T(8,128)(2,1)}), bf16[32,2,64,256]{3,2,1,0:T(8,128)(2,1)S(1)}, u32[]{:S(2)}, u32[]{:S(2)}) async-start(bf16[32,2,64,256]{3,2,1,0:T(8,128)(2,1)} %copy.44), calls=%async_computation.3 | async-start | bytes 4194304 | tf_op jit(solution)/shard_map/all_to_all | solution.py:108
  43.9 49.8 %copy-start.3 = (s32[20,6]{0,1:T(8,128)S(1)}, s32[20,6]{0,1:T(8,128)}, u32[]{:S(2)}) copy-start(s32[20,6]{0,1:T(8,128)} %param.14) | copy-start | bytes 1444
  43.9 50.0 %copy-start.1 = (bf16[320,512]{1,0:T(8,128)(2,1)S(1)}, bf16[320,512]{1,0:T(8,128)(2,1)}, u32[]{:S(2)}) copy-start(bf16[320,512]{1,0:T(8,128)(2,1)} %param.10) | copy-start | bytes 983044
  43.9 50.9 %copy-start.4 = (s32[20]{0:T(128)S(1)}, s32[20]{0:T(128)}, u32[]{:S(2)}) copy-start(s32[20]{0:T(128)} %param.13) | copy-start | bytes 244
  43.9 51.1 %copy-start.5 = (bf16[320,256]{1,0:T(8,128)(2,1)S(1)}, bf16[320,256]{1,0:T(8,128)(2,1)}, u32[]{:S(2)}) copy-start(bf16[320,256]{1,0:T(8,128)(2,1)} %param.11) | copy-start | bytes 491524
  87.7 100.6 %all-to-all-start.1 = ((bf16[32,2,64,512]{3,2,1,0:T(8,128)(2,1)}), bf16[32,2,64,512]{3,2,1,0:T(8,128)(2,1)}, u32[]{:S(2)}, u32[]{:S(2)}) async-start(bf16[32,2,64,512]{3,2,1,0:T(8,128)(2,1)} %copy.40), calls=%async_computation.2 | async-start | bytes 8388608 | tf_op jit(solution)/shard_map/all_to_all | solution.py:107
  93.5 151.9 %reduce-scatter.2.cloned.1.call-start = ((), (), s32[]{:S(2)}) async-start(), calls=%async_computation.4 | async-start | bytes 2785280 | tf_op jit(solution)/shard_map/reduce_scatter | solution.py:69
Sparse Core Ops, SparseCore 0:
  104.1 66.3 reduce-scatter.1
where the time goes:
time: 254 us
  waiting for transfers between devices  127 us (50%)
  blocking collectives  70.6 us (28%)
  matrix products  20.3 us (8%)
  between operations  13.6 us (5%)
  starting transfers between devices  11.2 us (4%)
  local copies, waits for them, and re-layouts  8.47 us (3%)
  other arithmetic  2.98 us (1%)
    all_to_all x1, waiting for transfers between devices, shards(): lax.all_to_all(down_blocks, 'rep', split_axis=0, concat_axis=0, tiled=True)  82.9 us
    psum x1, blocking collectives, shards(): down_projected = lax.psum(shrink_part.astype(jnp.bfloat16), 'tp')  49.5 us
    all_to_all x1, waiting for transfers between devices, shards(): lax.all_to_all(up_blocks, 'rep', split_axis=0, concat_axis=0, tiled=True)  43.8 us
    all_to_all x1, blocking collectives, shards(): lax.all_to_all(wanted, 'rep', split_axis=0, concat_axis=0, tiled=True)  21 us
    dot_general x1, matrix products, shards(): jnp.einsum('sr,skf->rkf', placing_mat, down_got, preferred_element_type=j...  6.75 us
    all_to_all x1, starting transfers between devices, shards(): lax.all_to_all(down_blocks, 'rep', split_axis=0, concat_axis=0, tiled=True)  5.76 us
    dot_general x1, matrix products, shards(): lax.dot_general(out_weight, attended, (((0,), (1,)), ((), ())), preferred...  5.37 us
    all_to_all x1, starting transfers between devices, shards(): lax.all_to_all(up_blocks, 'rep', split_axis=0, concat_axis=0, tiled=True)  5.2 us
  transfers between devices with their start and end apart: 3, of which 2 were waited for; matrix products, arithmetic and copies ran while one was open for 10% of the time, Pallas kernels for 0%

commit v1 on v0

--- a/solution.py
+++ b/solution.py
@@ -115,7 +115,7 @@
         "sr,skd->rkd", placing_mat, up_got, preferred_element_type=jnp.float32
     ).astype(jnp.bfloat16)
     shrink_part = jnp.einsum("rqf,rkf->rqk", by_row, down_sel, preferred_element_type=jnp.float32)
-    down_projected = lax.psum(shrink_part.astype(jnp.bfloat16), "tp")
+    down_projected = jnp.sum(lax.all_gather(shrink_part.astype(jnp.bfloat16), "tp"), axis=0)
     adapter_correction = jnp.einsum(
         "owe,oet->owt", down_projected, up_sel, preferred_element_type=jnp.float32
     ).astype(jnp.bfloat16)

time: 254 us -> 230 us (0.906)
  the two profiles are of different devices: /device:TPU:64 before, /device:TPU:1 now
where the time goes in v1:
time: 230 us; the launch traced here: 229 us
  waiting for transfers between devices  128 us (56%)
  blocking collectives  45.7 us (20%)
  matrix products  20.3 us (9%)
  between operations  13.6 us (6%)
  starting transfers between devices  10.6 us (5%)
  local copies, waits for them, and re-layouts  8.47 us (4%)
  other arithmetic  3.25 us (1%)
    all_to_all x1, waiting for transfers between devices, shards(): lax.all_to_all(down_blocks, 'rep', split_axis=0, concat_axis=0, tiled=True)  83.8 us
    all_to_all x1, waiting for transfers between devices, shards(): lax.all_to_all(up_blocks, 'rep', split_axis=0, concat_axis=0, tiled=True)  43.8 us
    all_gather x1, blocking collectives, shards(): lax.all_gather(shrink_part.astype(jnp.bfloat16), 'tp')  23.5 us
    all_to_all x1, blocking collectives, shards(): lax.all_to_all(wanted, 'rep', split_axis=0, concat_axis=0, tiled=True)  22.2 us
    dot_general x1, matrix products, shards(): jnp.einsum('sr,skf->rkf', placing_mat, down_got, preferred_element_type=j...  6.75 us
    all_to_all x1, starting transfers between devices, shards(): lax.all_to_all(down_blocks, 'rep', split_axis=0, concat_axis=0, tiled=True)  6.2 us
    dot_general x1, matrix products, shards(): lax.dot_general(out_weight, attended, (((0,), (1,)), ((), ())), preferred...  5.37 us
  transfers between devices with their start and end apart: 3, of which 2 were waited for; matrix products, arithmetic and copies ran while one was open for 11% of the time, Pallas kernels for 0%

profile of v1, /device:TPU:1, one launch (start us, length us, event | category | flops | bytes accessed | tf_op | source)
XLA Modules:
  0.0 229.5 jit_solution(10176671151164792861)
XLA Ops:
  6.5 0.0 copy-start
  6.5 0.9 select_reduce_fusion.1
  7.4 0.2 convert_reduce_fusion
  7.6 0.1 select_reduce_fusion
  7.7 0.1 sub.34
  7.8 22.2 %all_to_all.16 = s32[32,1,2]{2,1,0:T(1,128)S(1)} all-to-all(s32[32,1,2]{2,1,0:T(1,128)S(1)} %bitcast.64), channel_id=1, replica_groups=mesh['rep'=32,'tp'=16] {'rep'}, dimensions={0} | all-to-all | bytes 512 | tf_op jit(solution)/shard_map/all_to_all | solution.py:98
  30.0 0.1 copy.38
  30.1 1.6 convolution_convert_fusion.2
  31.7 2.5 %copy.44 = bf16[32,2,64,256]{3,2,1,0:T(8,128)(2,1)} copy(bf16[32,2,64,256]{3,0,2,1:T(8,128)(2,1)S(1)} %convolution_convert_fusion.2) | data formatting | bytes 4194304 | tf_op jit(solution)/shard_map/convert_element_type | solution.py:106
  34.2 0.0 copy-start.2
  34.2 4.1 %all-to-all-start.2 = ((bf16[32,2,64,256]{3,2,1,0:T(8,128)(2,1)}), bf16[32,2,64,256]{3,2,1,0:T(8,128)(2,1)S(1)}, u32[]{:S(2)}, u32[]{:S(2)}) async-start(bf16[32,2,64,256]{3,2,1,0:T(8,128)(2,1)} %copy.44), calls=%async_computation.3 | async-start | bytes 4194304 | tf_op jit(solution)/shard_map/all_to_all | solution.py:108
  38.4 0.0 copy-done.2
  38.4 1.3 convolution_convert_fusion.1
  39.7 4.3 %copy.40 = bf16[32,2,64,512]{3,2,1,0:T(8,128)(2,1)} copy(bf16[32,2,64,512]{3,0,2,1:T(8,128)(2,1)S(1)} %convolution_convert_fusion.1) | data formatting | bytes 8388608 | tf_op jit(solution)/shard_map/convert_element_type | solution.py:103
  44.0 0.0 copy-start.3
  44.0 0.0 copy-start.1
  44.0 0.0 copy-start.4
  44.0 0.0 copy-start.5
  44.0 43.8 %all-to-all-done.2 = bf16[32,2,64,256]{3,2,1,0:T(8,128)(2,1)S(1)} async-done(((bf16[32,2,64,256]{3,2,1,0:T(8,128)(2,1)}), bf16[32,2,64,256]{3,2,1,0:T(8,128)(2,1)S(1)}, u32[]{:S(2)}, u32[]{:S(2)}) %all-to-all-start.2) | async-done | bytes 2097184 | tf_op jit(solution)/shard_map/all_to_all | solution.py:108
  87.8 6.2 %all-to-all-start.1 = ((bf16[32,2,64,512]{3,2,1,0:T(8,128)(2,1)}), bf16[32,2,64,512]{3,2,1,0:T(8,128)(2,1)}, u32[]{:S(2)}, u32[]{:S(2)}) async-start(bf16[32,2,64,512]{3,2,1,0:T(8,128)(2,1)} %copy.40), calls=%async_computation.2 | async-start | bytes 8388608 | tf_op jit(solution)/shard_map/all_to_all | solution.py:107
  94.0 0.2 reduce-scatter.2.cloned.1.call-start
  94.3 0.0 copy-done.3
  94.3 0.1 copy.35
  94.4 0.1 reshape.210
  94.5 0.0 copy-done.1
  94.5 0.2 reshape.202
  94.7 0.0 copy-done
  94.7 0.7 gather_fusion
  95.4 0.0 copy-done.4
  95.4 0.1 iota_compare_fusion.3
  95.5 0.1 broadcast_compare_fusion
  95.6 0.0 copy-done.5
  95.6 0.4 fusion.56
  96.0 1.2 fusion.17
  97.2 1.7 convolution_convert_fusion.3
  98.9 0.2 reshape_transpose_reshape.4
  99.1 5.4 %fusion.1 = bf16[4096,320]{0,1:T(8,128)(2,1)} fusion(bf16[320,512]{1,0:T(8,128)(2,1)S(1)} %reshape_transpose_reshape.4, bf16[512,4096]{1,0:T(8,128)(2,1)} %param.15), kind=kOutput, calls=%fused_computation.3 | convolution fusion | flops 1343488000 | bytes 7143424 | tf_op jit(solution)/shard_map/dot_general | solution.py:70
  104.5 0.0 reduce-scatter.2.cloned.1.call-update
  104.5 0.2 reshape_reshape_transpose_reshape.3
  104.7 1.3 fusion.9
  106.0 83.8 %all-to-all-done.1 = bf16[32,2,64,512]{3,2,1,0:T(8,128)(2,1)} async-done(((bf16[32,2,64,512]{3,2,1,0:T(8,128)(2,1)}), bf16[32,2,64,512]{3,2,1,0:T(8,128)(2,1)}, u32[]{:S(2)}, u32[]{:S(2)}) %all-to-all-start.1) | async-done | bytes 4194336 | tf_op jit(solution)/shard_map/all_to_all | solution.py:107
  189.7 6.7 %fusion.6 = bf16[20,64,512]{2,0,1:T(8,128)(2,1)S(1)} fusion(bf16[64,64,512]{2,1,0:T(8,128)(2,1)} %bitcast.14, s32[20]{0:T(128)S(1)} %multiply_add_fusion), kind=kOutput, calls=%fused_computation.10 | convolution fusion | flops 84542720 | bytes 5505104 | tf_op jit(solution)/shard_map/sr,skf->rkf/dot_general | solution.py:111
  196.5 0.5 fusion.20
  197.0 23.5 %all-gather = bf16[320,16,64]{2,1,0:T(8,128)(2,1)S(1)} all-gather(bf16[20,16,64]{2,1,0:T(8,128)(2,1)S(1)} %fusion.20), channel_id=2, replica_groups=mesh['rep'=32,'tp'=16] {'tp'}, dimensions={0}, use_global_device_ids=true | all-gather | bytes 696320 | tf_op jit(solution)/shard_map/all_gather | solution.py:118
  220.5 0.3 reduce_sum.52
  220.8 0.2 fusion.19
  221.0 0.0 reduce-scatter.2.cloned.1.call-done
  221.0 1.6 fusion.30
  (7 shorter events, 0.0 us)
Async XLA Ops:
  6.5 88.2 %copy-start = (bf16[44,1,8,256]{3,2,1,0:T(8,128)(2,1)S(1)}, bf16[44,1,8,256]{3,2,1,0:T(8,128)(2,1)}, u32[]{:S(2)}) copy-start(bf16[44,1,8,256]{3,2,1,0:T(8,128)(2,1)} %param.12) | copy-start | bytes 540676
  34.2 4.2 %copy-start.2 = (bf16[2,64,512]{2,1,0:T(8,128)(2,1)S(1)}, bf16[2,64,512]{2,1,0:T(8,128)(2,1)}, u32[]{:S(2)}) copy-start(bf16[2,64,512]{2,1,0:T(8,128)(2,1)} %param.16) | copy-start | bytes 393220
  34.2 53.6 %all-to-all-start.2 = ((bf16[32,2,64,256]{3,2,1,0:T(8,128)(2,1)}), bf16[32,2,64,256]{3,2,1,0:T(8,128)(2,1)S(1)}, u32[]{:S(2)}, u32[]{:S(2)}) async-start(bf16[32,2,64,256]{3,2,1,0:T(8,128)(2,1)} %copy.44), calls=%async_computation.3 | async-start | bytes 4194304 | tf_op jit(solution)/shard_map/all_to_all | solution.py:108
  44.0 50.2 %copy-start.3 = (s32[20,6]{0,1:T(8,128)S(1)}, s32[20,6]{0,1:T(8,128)}, u32[]{:S(2)}) copy-start(s32[20,6]{0,1:T(8,128)} %param.14) | copy-start | bytes 1444
  44.0 50.5 %copy-start.1 = (bf16[320,512]{1,0:T(8,128)(2,1)S(1)}, bf16[320,512]{1,0:T(8,128)(2,1)}, u32[]{:S(2)}) copy-start(bf16[320,512]{1,0:T(8,128)(2,1)} %param.10) | copy-start | bytes 983044
  44.0 51.4 %copy-start.4 = (s32[20]{0:T(128)S(1)}, s32[20]{0:T(128)}, u32[]{:S(2)}) copy-start(s32[20]{0:T(128)} %param.13) | copy-start | bytes 244
  44.0 51.5 %copy-start.5 = (bf16[320,256]{1,0:T(8,128)(2,1)S(1)}, bf16[320,256]{1,0:T(8,128)(2,1)}, u32[]{:S(2)}) copy-start(bf16[320,256]{1,0:T(8,128)(2,1)} %param.11) | copy-start | bytes 491524
  87.8 101.9 %all-to-all-start.1 = ((bf16[32,2,64,512]{3,2,1,0:T(8,128)(2,1)}), bf16[32,2,64,512]{3,2,1,0:T(8,128)(2,1)}, u32[]{:S(2)}, u32[]{:S(2)}) async-start(bf16[32,2,64,512]{3,2,1,0:T(8,128)(2,1)} %copy.40), calls=%async_computation.2 | async-start | bytes 8388608 | tf_op jit(solution)/shard_map/all_to_all | solution.py:107
  94.0 127.0 %reduce-scatter.2.cloned.1.call-start = ((), (), s32[]{:S(2)}) async-start(), calls=%async_computation.4 | async-start | bytes 2785280 | tf_op jit(solution)/shard_map/reduce_scatter | solution.py:69
Sparse Core Ops, SparseCore 0:
  104.6 65.6 reduce-scatter.1
